TPU v7x, 256 devices: a whole 4x4x8 slice. The times are simulated.
256 devices in a mesh: dp: 16 (over x, y), expert: 16 (over z, core).
Axes of the slice: x: 4, y: 4, z: 8, core: 2. Of those that a mesh axis runs over, the one named last changes fastest.
Arguments:
- hidden: bfloat16 [32768, 8, 768], P(('dp', 'expert')), may hold values from -6 to 6
- upstream: bfloat16 [32768, 4096], P(('dp', 'expert')), may hold values from -0.125 to 0.125
- probs: bfloat16 [32768, 8], P(('dp', 'expert')), may hold values from 0.019897461 to 0.5
- expert_ids: int32 [32768, 8], P(('dp', 'expert')), may hold values from 0 to 15, all different within a row; in each aligned block of 128 rows (0 to 127, 128 to 255, ...) at most 72 rows name the same one
- w_down: bfloat16 [16, 4096, 768], P('expert', 'dp'), may hold values from -0.21875 to 0.21875
Outputs:
- grad_down: float32 [16, 4096, 768], P('expert', 'dp')
- gate_grad: float32 [32768, 8], P(('dp', 'expert'))
Inputs may be any that keep to these rules, and one draw needn't show every extreme that they name: `expert_ids`: each row names 8 different experts; among the rows of one device no expert is named by more than 72 rows, a bound that some block reaches.
All inputs are finite; a program needn't handle non-finite values.
Results may differ from a plain program's by a relative error of at most 0.013.
Values may be sent and summed in bfloat16 or wider, within the bound.
No kernel may reach another device: no remote copies, remote signals or barrier semaphores. Data moves between devices by JAX's collectives and lax.ppermute only.
A program may use at most 128 MiB of HBM per device.

v0:
```python
import jax
import jax.numpy as jnp
from jax import lax
from jax.sharding import Mesh, PartitionSpec as P


def body(hidden, upstream, probs, expert_ids, w_down):
    tok_rows, top_k = expert_ids.shape
    hid_width = hidden.shape[2]
    model_width = upstream.shape[1]
    lanes = 128
    n_z = lax.axis_size("z")
    n_core = lax.axis_size("core")
    groups = n_z * n_core
    n_dp = lax.axis_size("dp")
    slots_per = max(tok_rows * 9 // 16, tok_rows * top_k // groups)
    total_rows = groups * slots_per
    chosen = (expert_ids[:, :, None] == jnp.arange(groups, dtype=jnp.int32)[None, None, :]).astype(
        jnp.int32
    )
    member = jnp.sum(chosen, axis=1)
    slot_place = jnp.cumsum(member, axis=0) - 1
    which_k = jnp.sum(chosen * jnp.arange(top_k, dtype=jnp.int32)[None, :, None], axis=1)
    target = (
        (member == 1)[:, :, None]
        & (slot_place[:, :, None] == jnp.arange(slots_per, dtype=jnp.int32)[None, None, :])
    ).astype(jnp.int32)
    filled = jnp.sum(target, axis=0) == 1
    source_tok = jnp.sum(target * jnp.arange(tok_rows, dtype=jnp.int32)[:, None, None], axis=0)
    source_k = jnp.sum(target * which_k[:, :, None], axis=0)
    flat_index = (source_tok * top_k + source_k).reshape(-1)
    picked_h = hidden.reshape(tok_rows * top_k, hid_width)[flat_index].reshape(
        groups, slots_per, hid_width
    )
    send_h = jnp.where(filled[:, :, None], picked_h, jnp.zeros_like(picked_h))
    picked_p = probs.reshape(-1)[flat_index].reshape(groups, slots_per)
    send_p = jnp.where(filled, picked_p, jnp.zeros_like(picked_p))
    dy3 = upstream.reshape(tok_rows, model_width // lanes, lanes)
    dy_z = lax.all_gather(dy3, "z", axis=0, tiled=True)
    dy_pair = lax.ppermute(dy_z, "core", perm=[(c, (c + 1) % n_core) for c in range(n_core)])
    dy_all = jnp.concatenate([dy_z, dy_pair], axis=0)
    w_blocks = lax.all_to_all(
        jnp.broadcast_to(w_down, (n_dp,) + w_down.shape[1:]),
        "dp",
        split_axis=0,
        concat_axis=0,
        tiled=True,
    )
    w_full = w_blocks.reshape(n_dp * w_down.shape[1] // lanes, lanes, hid_width)
    ez = ("z", "core")
    recv_h, recv_p, recv_tok = (
        lax.all_to_all(send_h, ez, split_axis=0, concat_axis=0, tiled=True),
        lax.all_to_all(send_p, ez, split_axis=0, concat_axis=0, tiled=True),
        lax.all_to_all(source_tok, ez, split_axis=0, concat_axis=0, tiled=True),
    )
    src = jnp.arange(groups, dtype=jnp.int32)
    src_z, src_core = (src // n_core, src % n_core)
    my_core = lax.axis_index("core")
    block = (src_core - my_core + n_core) % n_core
    row_of = recv_tok + (tok_rows * (block * n_z + src_z))[:, None]
    rows_h = recv_h.reshape(total_rows, hid_width)
    rows_dy = dy_all[row_of.reshape(-1)]
    projected = lax.dot_general(
        rows_h, w_full, (((1,), (2,)), ((), ())), preferred_element_type=jnp.float32
    )
    scores = jnp.sum(projected * rows_dy.astype(jnp.float32), axis=(1, 2))
    returned = lax.all_to_all(
        scores.reshape(groups, slots_per), ez, split_axis=0, concat_axis=0, tiled=True
    )
    scaled = (
        recv_p.reshape(total_rows, 1, 1).astype(jnp.float32) * rows_dy.astype(jnp.float32)
    ).astype(jnp.bfloat16)
    partial = lax.dot_general(
        scaled, rows_h, (((0,), (0,)), ((), ())), preferred_element_type=jnp.float32
    ).astype(jnp.bfloat16)
    grad_block = lax.psum_scatter(
        partial.reshape(model_width, hid_width), "dp", scatter_dimension=0, tiled=True
    ).astype(jnp.float32)
    place_slot = jnp.take_along_axis(slot_place, expert_ids, axis=1)
    gate_grad = returned[expert_ids, place_slot]
    return (grad_block[None], gate_grad)


def solution(mesh):
    n_dp, n_expert = mesh.devices.shape
    sub = Mesh(mesh.devices.reshape(n_dp, n_expert // 2, 2), ("dp", "z", "core"))
    tok = ("dp", "z", "core")
    in_specs = (
        P(tok, None, None),
        P(tok, None),
        P(tok, None),
        P(tok, None),
        P(("z", "core"), "dp", None),
    )
    out_specs = (P(("z", "core"), "dp", None), P(tok, None))
    return jax.shard_map(body, mesh=sub, in_specs=in_specs, out_specs=out_specs, check_vma=False)
```

profile of v0, /device:TPU:1, one launch (start us, length us, event | category | flops | bytes accessed | tf_op | source)
XLA Modules:
  0.0 389.1 jit_solution(15925728178710582814)
XLA Ops:
  7.2 2.6 copy.58
  9.8 98.1 %all-gather.2.cloned.1.call-done = bf16[1024,32,128]{2,1,0:T(8,128)(2,1)} async-done(((bf16[128,32,128]{2,1,0:T(8,128)(2,1)}), bf16[1024,32,128]{2,1,0:T(8,128)(2,1)}) %all-gather.2.cloned.1.call-update) | async-done | bytes 8388624 | tf_op jit(solution)/shard_map/all_gather | solution.py:39
  109.6 1.5 convert_reduce_fusion
  112.9 7.3 %gather_fusion = bf16[1152]{0:T(1024)(128)(2,1)S(1)} fusion(bf16[1024]{0:T(1024)(128)(2,1)S(1)} %reshape.188, s32[2048]{0:T(1024)S(1)} %pad_clamp_fusion.1), kind=kCustom, calls=%fused_computation | custom fusion | bytes 9216 | tf_op jit(solution)/shard_map/gather | solution.py:36
  120.9 4.4 %all-to-all-start = ((bf16[16,1,72]{2,1,0:T(2,128)(2,1)}), bf16[16,1,72]{2,1,0:T(2,128)(2,1)S(1)}, u32[]{:S(2)}, u32[]{:S(2)}) async-start(bf16[16,1,72]{2,1,0:T(2,128)(2,1)} %copy.51), calls=%async_computation | async-start | bytes 16384 | tf_op jit(solution)/shard_map/all_to_all | solution.py:53
  125.3 4.6 %gather_fusion.2 = bf16[1152,768]{1,0:T(8,128)(2,1)S(1)} fusion(bf16[1024,768]{1,0:T(8,128)(2,1)S(1)} %bitcast.26, s32[2048]{0:T(1024)S(1)} %pad_clamp_fusion.1), kind=kCustom, calls=%fused_computation.2 | custom fusion | bytes 3543552 | tf_op jit(solution)/shard_map/gather | solution.py:32
  129.9 2.5 all-to-all-done
  132.3 4.8 %all-to-all-start.1 = ((s32[16,1,72]{2,1,0:T(1,128)}), s32[16,1,72]{2,1,0:T(1,128)S(1)}, u32[]{:S(2)}, u32[]{:S(2)}) async-start(s32[16,1,72]{2,1,0:T(1,128)} %bitcast.2), calls=%async_computation.1 | async-start | bytes 16384 | tf_op jit(solution)/shard_map/all_to_all | solution.py:54
  138.6 5.5 %all-to-all-done.1 = s32[16,1,72]{2,1,0:T(1,128)S(1)} async-done(((s32[16,1,72]{2,1,0:T(1,128)}), s32[16,1,72]{2,1,0:T(1,128)S(1)}, u32[]{:S(2)}, u32[]{:S(2)}) %all-to-all-start.1) | async-done | bytes 4640 | tf_op jit(solution)/shard_map/all_to_all | solution.py:54
  144.1 4.2 %all-to-all-start.2 = ((bf16[16,72,768]{2,1,0:T(8,128)(2,1)}), bf16[16,72,768]{2,1,0:T(8,128)(2,1)S(1)}, u32[]{:S(2)}, u32[]{:S(2)}) async-start(bf16[16,72,768]{2,1,0:T(8,128)(2,1)} %broadcast_select_fusion), calls=%async_computation.2 | async-start | bytes 3538944 | tf_op jit(solution)/shard_map/all_to_all | solution.py:52
  149.9 16.7 %pad_maximum_fusion = bf16[2048,32,128]{2,1,0:T(8,128)(2,1)} fusion(bf16[1024,32,128]{2,1,0:T(8,128)(2,1)} %collective-permute-done, bf16[1024,32,128]{2,1,0:T(8,128)(2,1)} %all-gather.2.cloned.1.call-done), kind=kLoop, calls=%fused_computation.8 | loop fusion | flops 8388608 | bytes 33554432 | tf_op jit(solution)/shard_map/concatenate | solution.py:41
  166.6 11.8 %gather_fusion.1 = bf16[1152,32,128]{2,1,0:T(8,128)(2,1)} fusion(bf16[2048,32,128]{2,1,0:T(8,128)(2,1)} %pad_maximum_fusion, s32[2048]{0:T(1024)S(1)} %pad_clamp_fusion), kind=kCustom, calls=%fused_computation.1 | custom fusion | bytes 18878976 | tf_op jit(solution)/shard_map/gather | solution.py:62
  178.4 12.9 %copy.53 = bf16[1152,32,128]{0,2,1:T(8,128)(2,1)} copy(bf16[1152,32,128]{2,1,0:T(8,128)(2,1)} %gather_fusion.1) | data formatting | bytes 18874368 | tf_op jit(solution)/shard_map/gather | solution.py:62
  191.3 14.0 %fusion.5 = bf16[32,128,768]{2,1,0:T(8,128)(2,1)} fusion(bf16[1152,768,1]{1,0,2:T(8,128)(2,1)S(1)} %bitcast.31, bf16[1152,32,128]{0,2,1:T(8,128)(2,1)} %copy.53, f32[1152]{0:T(1024)S(1)} %reshape.196), kind=kOutput, calls=%fused_computation.12 | convolution fusion | flops 7265058816 | bytes 17502720 | tf_op jit(solution)/shard_map/dot_general | solution.py:73
  205.4 3.3 broadcast_in_dim.54
  208.7 6.6 %all-to-all-start.3 = ((bf16[16,256,768]{2,1,0:T(8,128)(2,1)}), bf16[16,256,768]{2,1,0:T(8,128)(2,1)}, u32[]{:S(2)}, u32[]{:S(2)}) async-start(bf16[16,256,768]{2,1,0:T(8,128)(2,1)} %broadcast_in_dim.54), calls=%async_computation.4 | async-start | bytes 12582912 | tf_op jit(solution)/shard_map/all_to_all | solution.py:42
  215.5 7.1 %gather_fusion.4 = s32[1024]{0:T(1024)S(1)} fusion(s32[128,16]{1,0:T(8,128)S(1)} %broadcast_add_fusion, s32[1024]{0:T(1024)S(1)} %reshape.228), kind=kCustom, calls=%fused_computation.4 | custom fusion | bytes 16384 | tf_op jit(solution)/shard_map/jit(take_along_axis)/gather | solution.py:79
  222.7 107.3 %all-to-all-done.3 = bf16[16,256,768]{2,1,0:T(8,128)(2,1)} async-done(((bf16[16,256,768]{2,1,0:T(8,128)(2,1)}), bf16[16,256,768]{2,1,0:T(8,128)(2,1)}, u32[]{:S(2)}, u32[]{:S(2)}) %all-to-all-start.3) | async-done | bytes 6291488 | tf_op jit(solution)/shard_map/all_to_all | solution.py:42
  330.0 14.2 %fusion.4 = f32[1152]{0:T(1024)S(1)} fusion(bf16[1152,32,128]{0,2,1:T(8,128)(2,1)} %copy.53, bf16[1152,768,1]{1,0,2:T(8,128)(2,1)S(1)} %bitcast.32, bf16[32,128,768]{2,1,0:T(8,128)(2,1)} %bitcast.11), kind=kOutput, calls=%fused_computation.11 | convolution fusion | flops 7261912064 | bytes 17502720 | tf_op jit(solution)/shard_map/dot_general | solution.py:63
  344.9 7.1 %all-to-all-start.4 = ((f32[16,1,72]{2,1,0:T(1,128)}), f32[16,1,72]{2,1,0:T(1,128)S(1)}, u32[]{:S(2)}, u32[]{:S(2)}) async-start(f32[16,1,72]{2,1,0:T(1,128)} %all_to_all.32), calls=%async_computation.5 | async-start | bytes 16384 | tf_op jit(solution)/shard_map/all_to_all | solution.py:67
  352.2 6.7 %all-to-all-done.4 = f32[16,1,72]{2,1,0:T(1,128)S(1)} async-done(((f32[16,1,72]{2,1,0:T(1,128)}), f32[16,1,72]{2,1,0:T(1,128)S(1)}, u32[]{:S(2)}, u32[]{:S(2)}) %all-to-all-start.4) | async-done | bytes 4640 | tf_op jit(solution)/shard_map/all_to_all | solution.py:67
  358.9 6.8 %gather_fusion.3 = f32[1024]{0:T(1024)S(1)} fusion(f32[16,72]{1,0:T(8,128)S(1)} %bitcast.27, s32[1024]{0:T(1024)S(1)} %reshape.222), kind=kCustom, calls=%fused_computation.3 | custom fusion | bytes 16384 | tf_op jit(solution)/shard_map/gather | solution.py:80
  366.4 13.9 %reduce-scatter.2.cloned.1.call-done = bf16[256,768]{1,0:T(8,128)(2,1)} async-done(((bf16[4096,768]{1,0:T(8,128)(2,1)}), bf16[256,768]{1,0:T(8,128)(2,1)}) %reduce-scatter.2.cloned.1.call-update) | async-done | bytes 393232 | tf_op jit(solution)/shard_map/reduce_scatter | solution.py:76
  380.4 1.9 bitcast_convert_fusion
  (52 shorter events, 9.3 us)
Async XLA Ops:
  7.2 118.2 %copy-start = (bf16[128,8,768]{2,1,0:T(8,128)(2,1)S(1)}, bf16[128,8,768]{2,1,0:T(8,128)(2,1)}, u32[]{:S(2)}) copy-start(bf16[128,8,768]{2,1,0:T(8,128)(2,1)} %param.5) | copy-start | bytes 4718596
  7.2 100.7 %all-gather.2.cloned.1.call-start = ((), (), s32[]{:S(2)}) async-start(), calls=%async_computation.6 | async-start | bytes 9437184 | tf_op jit(solution)/shard_map/all_gather | solution.py:39
  107.9 42.0 %collective-permute-start = (bf16[1024,32,128]{2,1,0:T(8,128)(2,1)}, bf16[1024,32,128]{2,1,0:T(8,128)(2,1)}, u32[]{:S(2)}, u32[]{:S(2)}) collective-permute-start(bf16[1024,32,128]{2,1,0:T(8,128)(2,1)} %all-gather.2.cloned.1.call-done), channel_id=1, source_target_pairs={{0,1},{1,0},{2,3},{3,2},{4,5},{5,4},{6,7},{7,6},{8,9},{9,8},{10,11... | collective-permute-start | bytes 25165832 | tf_op jit(solution)/shard_map/ppermute | solution.py:40
  120.9 11.5 %all-to-all-start = ((bf16[16,1,72]{2,1,0:T(2,128)(2,1)}), bf16[16,1,72]{2,1,0:T(2,128)(2,1)S(1)}, u32[]{:S(2)}, u32[]{:S(2)}) async-start(bf16[16,1,72]{2,1,0:T(2,128)(2,1)} %copy.51), calls=%async_computation | async-start | bytes 16384 | tf_op jit(solution)/shard_map/all_to_all | solution.py:53
  132.3 11.7 %all-to-all-start.1 = ((s32[16,1,72]{2,1,0:T(1,128)}), s32[16,1,72]{2,1,0:T(1,128)S(1)}, u32[]{:S(2)}, u32[]{:S(2)}) async-start(s32[16,1,72]{2,1,0:T(1,128)} %bitcast.2), calls=%async_computation.1 | async-start | bytes 16384 | tf_op jit(solution)/shard_map/all_to_all | solution.py:54
  144.1 47.3 %all-to-all-start.2 = ((bf16[16,72,768]{2,1,0:T(8,128)(2,1)}), bf16[16,72,768]{2,1,0:T(8,128)(2,1)S(1)}, u32[]{:S(2)}, u32[]{:S(2)}) async-start(bf16[16,72,768]{2,1,0:T(8,128)(2,1)} %broadcast_select_fusion), calls=%async_computation.2 | async-start | bytes 3538944 | tf_op jit(solution)/shard_map/all_to_all | solution.py:52
  148.2 232.1 %reduce-scatter.2.cloned.1.call-start = ((), (), s32[]{:S(2)}) async-start(), calls=%async_computation.7 | async-start | bytes 6684672 | tf_op jit(solution)/shard_map/reduce_scatter | solution.py:76
  191.3 14.0 %copy-start.2 = (bf16[1,256,768]{2,1,0:T(8,128)(2,1)S(1)}, bf16[1,256,768]{2,1,0:T(8,128)(2,1)}, u32[]{:S(2)}) copy-start(bf16[1,256,768]{2,1,0:T(8,128)(2,1)} %param.9) | copy-start | bytes 1179652
  205.3 9.9 %copy-start.3 = (s32[128,8]{0,1:T(8,128)S(1)}, s32[128,8]{0,1:T(8,128)}, u32[]{:S(2)}) copy-start(s32[128,8]{0,1:T(8,128)} %param.8) | copy-start | bytes 12292
  208.7 121.3 %all-to-all-start.3 = ((bf16[16,256,768]{2,1,0:T(8,128)(2,1)}), bf16[16,256,768]{2,1,0:T(8,128)(2,1)}, u32[]{:S(2)}, u32[]{:S(2)}) async-start(bf16[16,256,768]{2,1,0:T(8,128)(2,1)} %broadcast_in_dim.54), calls=%async_computation.4 | async-start | bytes 12582912 | tf_op jit(solution)/shard_map/all_to_all | solution.py:42
  344.9 14.0 %all-to-all-start.4 = ((f32[16,1,72]{2,1,0:T(1,128)}), f32[16,1,72]{2,1,0:T(1,128)S(1)}, u32[]{:S(2)}, u32[]{:S(2)}) async-start(f32[16,1,72]{2,1,0:T(1,128)} %all_to_all.32), calls=%async_computation.5 | async-start | bytes 16384 | tf_op jit(solution)/shard_map/all_to_all | solution.py:67
  358.9 23.4 %copy-start.1 = (bf16[128,8,768]{2,1,0:T(8,128)(2,1)S(1)}, bf16[128,8,768]{2,1,0:T(8,128)(2,1)}, u32[]{:S(2)}) copy-start(bf16[128,8,768]{2,1,0:T(8,128)(2,1)} %param.5) | copy-start | bytes 4718596
Sparse Core Ops, SparseCore 0:
  9.9 97.9 all-gather.1
  205.5 174.8 reduce-scatter.1
where the time goes:
time: 390 us; the launch traced here: 389 us
  waiting for transfers between devices  234 us (60%)
  local copies, waits for them, and re-layouts  60.9 us (16%)
  matrix products  28.2 us (7%)
  starting transfers between devices  27.8 us (7%)
  other arithmetic  24 us (6%)
  between operations  14.2 us (4%)
    all_to_all x1, waiting for transfers between devices, body(): lax.all_to_all(jnp.broadcast_to(w_down, (n_dp,) + w_down.shape[1:]), 'dp'...  107 us
    all_gather x1, waiting for transfers between devices, body(): dy_z = lax.all_gather(dy3, 'z', axis=0, tiled=True)  98.1 us
    gather x2, local copies, waits for them, and re-layouts, body(): rows_dy = dy_all[row_of.reshape(-1)]  24.7 us
    concatenate x1, other arithmetic, body(): dy_all = jnp.concatenate([dy_z, dy_pair], axis=0)  16.7 us
    dot_general x1, matrix products, body(): lax.dot_general(rows_h, w_full, (((1,), (2,)), ((), ())), preferred_eleme...  14.2 us
    dot_general x1, matrix products, body(): lax.dot_general(scaled, rows_h, (((0,), (0,)), ((), ())), preferred_eleme...  14 us
    reduce_scatter x1, waiting for transfers between devices, body(): lax.psum_scatter(partial.reshape(model_width, hid_width), 'dp', scatter_d...  13.9 us
  transfers between devices with their start and end apart: 8, of which 6 were waited for; matrix products, arithmetic and copies ran while one was open for 24% of the time, Pallas kernels for 0%

commit v1 on v0

--- a/solution.py
+++ b/solution.py
@@ -36,7 +36,15 @@
     picked_p = probs.reshape(-1)[flat_index].reshape(groups, slots_per)
     send_p = jnp.where(filled, picked_p, jnp.zeros_like(picked_p))
     dy3 = upstream.reshape(tok_rows, model_width // lanes, lanes)
-    dy_z = lax.all_gather(dy3, "z", axis=0, tiled=True)
+    dy_z = jnp.concatenate(
+        lax.all_to_all(
+            jnp.stack([dy3] * lax.axis_size("z"), axis=0),
+            axis_name="z",
+            split_axis=0,
+            concat_axis=0,
+        ),
+        0,
+    )
     dy_pair = lax.ppermute(dy_z, "core", perm=[(c, (c + 1) % n_core) for c in range(n_core)])
     dy_all = jnp.concatenate([dy_z, dy_pair], axis=0)
     w_blocks = lax.all_to_all(

time: 390 us -> 486 us (1.25)
  blocking collectives: 0 us -> 193 us
  waiting for transfers between devices: 234 us -> 136 us
    all_to_all x0 -> x1, blocking collectives: none -> 193 us  [body(): lax.all_to_all(jnp.stack([dy3] * lax.axis_size('z'), axis=0), axis_name='...]
    all_gather x1 -> x0, waiting for transfers between devices: 98.1 us -> none  [body(): dy_z = lax.all_gather(dy3, 'z', axis=0, tiled=True)]
  transfers between devices with their start and end apart: 8 -> 7, of which waited for: 6 -> 5; matrix products, arithmetic and copies ran while one was open for 24% -> 19% of each run, Pallas kernels for 0% -> 0%
where the time goes in v1:
time: 486 us; the launch traced here: 485 us
  blocking collectives  193 us (40%)
  waiting for transfers between devices  136 us (28%)
  local copies, waits for them, and re-layouts  60.7 us (12%)
  starting transfers between devices  28.6 us (6%)
  matrix products  28.2 us (6%)
  other arithmetic  23.3 us (5%)
  between operations  14.3 us (3%)
    all_to_all x1, blocking collectives, body(): lax.all_to_all(jnp.stack([dy3] * lax.axis_size('z'), axis=0), axis_name='...  193 us
    all_to_all x1, waiting for transfers between devices, body(): lax.all_to_all(jnp.broadcast_to(w_down, (n_dp,) + w_down.shape[1:]), 'dp'...  107 us
    gather x2, local copies, waits for them, and re-layouts, body(): rows_dy = dy_all[row_of.reshape(-1)]  24.7 us
    concatenate x1, other arithmetic, body(): dy_all = jnp.concatenate([dy_z, dy_pair], axis=0)  16.7 us
    dot_general x1, matrix products, body(): lax.dot_general(rows_h, w_full, (((1,), (2,)), ((), ())), preferred_eleme...  14.2 us
    reduce_scatter x1, waiting for transfers between devices, body(): lax.psum_scatter(partial.reshape(model_width, hid_width), 'dp', scatter_d...  14.1 us
    dot_general x1, matrix products, body(): lax.dot_general(scaled, rows_h, (((0,), (0,)), ((), ())), preferred_eleme...  14 us
  transfers between devices with their start and end apart: 7, of which 5 were waited for; matrix products, arithmetic and copies ran while one was open for 19% of the time, Pallas kernels for 0%

profile of v1, /device:TPU:1, one launch (start us, length us, event | category | flops | bytes accessed | tf_op | source)
XLA Modules:
  0.0 484.6 jit_solution(4995638491623192618)
XLA Ops:
  7.2 1.6 copy.58
  10.2 193.4 %all_to_all.45 = bf16[8,128,32,128]{3,2,1,0:T(8,128)(2,1)} all-to-all(bf16[8,128,32,128]{3,2,1,0:T(8,128)(2,1)S(1)} %stack.3), channel_id=1, replica_groups=mesh['dp'=16,'z'=8,'core'=2] {'z'}, dimensions={0} | all-to-all | bytes 16777216 | tf_op jit(solution)/shard_map/all_to_all | solution.py:40
  203.7 2.5 collective-permute-start
  209.1 7.3 %gather_fusion = bf16[1152]{0:T(1024)(128)(2,1)S(1)} fusion(bf16[1024]{0:T(1024)(128)(2,1)S(1)} %reshape.190, s32[2048]{0:T(1024)S(1)} %pad_clamp_fusion.1), kind=kCustom, calls=%fused_computation | custom fusion | bytes 9216 | tf_op jit(solution)/shard_map/gather | solution.py:36
  217.1 3.3 all-to-all-start
  220.4 4.6 gather_fusion.2
  224.9 2.5 all-to-all-done
  227.4 4.8 all-to-all-start.2
  233.6 5.5 %all-to-all-done.2 = s32[16,1,72]{2,1,0:T(1,128)S(1)} async-done(((s32[16,1,72]{2,1,0:T(1,128)}), s32[16,1,72]{2,1,0:T(1,128)S(1)}, u32[]{:S(2)}, u32[]{:S(2)}) %all-to-all-start.2) | async-done | bytes 4640 | tf_op jit(solution)/shard_map/all_to_all | solution.py:62
  239.2 4.2 all-to-all-start.3
  245.0 16.7 %pad_maximum_fusion = bf16[2048,32,128]{2,1,0:T(8,128)(2,1)} fusion(bf16[1024,32,128]{2,1,0:T(8,128)(2,1)} %collective-permute-done, bf16[1024,32,128]{2,1,0:T(8,128)(2,1)} %bitcast.1), kind=kLoop, calls=%fused_computation.8 | loop fusion | flops 8388608 | bytes 33554432 | tf_op jit(solution)/shard_map/concatenate | solution.py:49
  261.7 11.8 %gather_fusion.1 = bf16[1152,32,128]{2,1,0:T(8,128)(2,1)} fusion(bf16[2048,32,128]{2,1,0:T(8,128)(2,1)} %pad_maximum_fusion, s32[2048]{0:T(1024)S(1)} %pad_clamp_fusion), kind=kCustom, calls=%fused_computation.1 | custom fusion | bytes 18878976 | tf_op jit(solution)/shard_map/gather | solution.py:70
  273.5 12.9 %copy.53 = bf16[1152,32,128]{0,2,1:T(8,128)(2,1)} copy(bf16[1152,32,128]{2,1,0:T(8,128)(2,1)} %gather_fusion.1) | data formatting | bytes 18874368 | tf_op jit(solution)/shard_map/gather | solution.py:70
  286.4 14.0 %fusion.5 = bf16[32,128,768]{2,1,0:T(8,128)(2,1)} fusion(bf16[1152,768,1]{1,0,2:T(8,128)(2,1)S(1)} %bitcast.32, bf16[1152,32,128]{0,2,1:T(8,128)(2,1)} %copy.53, f32[1152]{0:T(1024)S(1)} %reshape.198), kind=kOutput, calls=%fused_computation.12 | convolution fusion | flops 7265058816 | bytes 17502720 | tf_op jit(solution)/shard_map/dot_general | solution.py:81
  300.4 3.3 broadcast_in_dim.54
  303.7 6.8 %all-to-all-start.4 = ((bf16[16,256,768]{2,1,0:T(8,128)(2,1)}), bf16[16,256,768]{2,1,0:T(8,128)(2,1)}, u32[]{:S(2)}, u32[]{:S(2)}) async-start(bf16[16,256,768]{2,1,0:T(8,128)(2,1)} %broadcast_in_dim.54), calls=%async_computation.5 | async-start | bytes 12582912 | tf_op jit(solution)/shard_map/all_to_all | solution.py:50
  310.8 7.1 %gather_fusion.4 = s32[1024]{0:T(1024)S(1)} fusion(s32[128,16]{1,0:T(8,128)S(1)} %broadcast_add_fusion, s32[1024]{0:T(1024)S(1)} %reshape.230), kind=kCustom, calls=%fused_computation.4 | custom fusion | bytes 16384 | tf_op jit(solution)/shard_map/jit(take_along_axis)/gather | solution.py:87
  318.0 107.3 %all-to-all-done.4 = bf16[16,256,768]{2,1,0:T(8,128)(2,1)} async-done(((bf16[16,256,768]{2,1,0:T(8,128)(2,1)}), bf16[16,256,768]{2,1,0:T(8,128)(2,1)}, u32[]{:S(2)}, u32[]{:S(2)}) %all-to-all-start.4) | async-done | bytes 6291488 | tf_op jit(solution)/shard_map/all_to_all | solution.py:50
  425.3 14.2 %fusion.4 = f32[1152]{0:T(1024)S(1)} fusion(bf16[1152,32,128]{0,2,1:T(8,128)(2,1)} %copy.53, bf16[1152,768,1]{1,0,2:T(8,128)(2,1)S(1)} %bitcast.33, bf16[32,128,768]{2,1,0:T(8,128)(2,1)} %bitcast.12), kind=kOutput, calls=%fused_computation.11 | convolution fusion | flops 7261912064 | bytes 17502720 | tf_op jit(solution)/shard_map/dot_general | solution.py:71
  440.2 7.1 %all-to-all-start.5 = ((f32[16,1,72]{2,1,0:T(1,128)}), f32[16,1,72]{2,1,0:T(1,128)S(1)}, u32[]{:S(2)}, u32[]{:S(2)}) async-start(f32[16,1,72]{2,1,0:T(1,128)} %all_to_all.36), calls=%async_computation.6 | async-start | bytes 16384 | tf_op jit(solution)/shard_map/all_to_all | solution.py:75
  447.4 6.7 %all-to-all-done.5 = f32[16,1,72]{2,1,0:T(1,128)S(1)} async-done(((f32[16,1,72]{2,1,0:T(1,128)}), f32[16,1,72]{2,1,0:T(1,128)S(1)}, u32[]{:S(2)}, u32[]{:S(2)}) %all-to-all-start.5) | async-done | bytes 4640 | tf_op jit(solution)/shard_map/all_to_all | solution.py:75
  454.2 6.8 %gather_fusion.3 = f32[1024]{0:T(1024)S(1)} fusion(f32[16,72]{1,0:T(8,128)S(1)} %bitcast.28, s32[1024]{0:T(1024)S(1)} %reshape.224), kind=kCustom, calls=%fused_computation.3 | custom fusion | bytes 16384 | tf_op jit(solution)/shard_map/gather | solution.py:88
  461.7 14.1 %reduce-scatter.2.cloned.1.call-done = bf16[256,768]{1,0:T(8,128)(2,1)} async-done(((bf16[4096,768]{1,0:T(8,128)(2,1)}), bf16[256,768]{1,0:T(8,128)(2,1)}) %reduce-scatter.2.cloned.1.call-update) | async-done | bytes 393232 | tf_op jit(solution)/shard_map/reduce_scatter | solution.py:84
  475.9 1.9 bitcast_convert_fusion
  (53 shorter events, 10.1 us)
Async XLA Ops:
  7.2 213.2 %copy-start = (bf16[128,8,768]{2,1,0:T(8,128)(2,1)S(1)}, bf16[128,8,768]{2,1,0:T(8,128)(2,1)}, u32[]{:S(2)}) copy-start(bf16[128,8,768]{2,1,0:T(8,128)(2,1)} %param.5) | copy-start | bytes 4718596
  10.2 195.9 %copy-start.3 = (s32[128,8]{0,1:T(8,128)S(1)}, s32[128,8]{0,1:T(8,128)}, u32[]{:S(2)}) copy-start(s32[128,8]{0,1:T(8,128)} %param.8) | copy-start | bytes 12292
  10.2 198.6 %copy-start.4 = (bf16[128,8]{0,1:T(8,128)(2,1)S(1)}, bf16[128,8]{0,1:T(8,128)(2,1)}, u32[]{:S(2)}) copy-start(bf16[128,8]{0,1:T(8,128)(2,1)} %param.7) | copy-start | bytes 6148
  203.7 41.3 %collective-permute-start = (bf16[1024,32,128]{2,1,0:T(8,128)(2,1)}, bf16[1024,32,128]{2,1,0:T(8,128)(2,1)}, u32[]{:S(2)}, u32[]{:S(2)}) collective-permute-start(bf16[1024,32,128]{2,1,0:T(8,128)(2,1)} %bitcast.1), channel_id=1, source_target_pairs={{0,1},{1,0},{2,3},{3,2},{4,5},{5,4},{6,7},{7,6},{8,9},{9,8},{10,11... | collective-permute-start | bytes 25165832 | tf_op jit(solution)/shard_map/ppermute | solution.py:48
  217.1 10.3 %all-to-all-start = ((bf16[16,1,72]{2,1,0:T(2,128)(2,1)}), bf16[16,1,72]{2,1,0:T(2,128)(2,1)S(1)}, u32[]{:S(2)}, u32[]{:S(2)}) async-start(bf16[16,1,72]{2,1,0:T(2,128)(2,1)} %copy.51), calls=%async_computation | async-start | bytes 16384 | tf_op jit(solution)/shard_map/all_to_all | solution.py:61
  227.4 11.7 %all-to-all-start.2 = ((s32[16,1,72]{2,1,0:T(1,128)}), s32[16,1,72]{2,1,0:T(1,128)S(1)}, u32[]{:S(2)}, u32[]{:S(2)}) async-start(s32[16,1,72]{2,1,0:T(1,128)} %bitcast.3), calls=%async_computation.2 | async-start | bytes 16384 | tf_op jit(solution)/shard_map/all_to_all | solution.py:62
  239.2 47.3 %all-to-all-start.3 = ((bf16[16,72,768]{2,1,0:T(8,128)(2,1)}), bf16[16,72,768]{2,1,0:T(8,128)(2,1)S(1)}, u32[]{:S(2)}, u32[]{:S(2)}) async-start(bf16[16,72,768]{2,1,0:T(8,128)(2,1)} %broadcast_select_fusion), calls=%async_computation.3 | async-start | bytes 3538944 | tf_op jit(solution)/shard_map/all_to_all | solution.py:60
  243.3 232.5 %reduce-scatter.2.cloned.1.call-start = ((), (), s32[]{:S(2)}) async-start(), calls=%async_computation.7 | async-start | bytes 6684672 | tf_op jit(solution)/shard_map/reduce_scatter | solution.py:84
  286.4 14.0 %copy-start.2 = (bf16[1,256,768]{2,1,0:T(8,128)(2,1)S(1)}, bf16[1,256,768]{2,1,0:T(8,128)(2,1)}, u32[]{:S(2)}) copy-start(bf16[1,256,768]{2,1,0:T(8,128)(2,1)} %param.9) | copy-start | bytes 1179652
  303.7 121.5 %all-to-all-start.4 = ((bf16[16,256,768]{2,1,0:T(8,128)(2,1)}), bf16[16,256,768]{2,1,0:T(8,128)(2,1)}, u32[]{:S(2)}, u32[]{:S(2)}) async-start(bf16[16,256,768]{2,1,0:T(8,128)(2,1)} %broadcast_in_dim.54), calls=%async_computation.5 | async-start | bytes 12582912 | tf_op jit(solution)/shard_map/all_to_all | solution.py:50
  440.2 14.0 %all-to-all-start.5 = ((f32[16,1,72]{2,1,0:T(1,128)}), f32[16,1,72]{2,1,0:T(1,128)S(1)}, u32[]{:S(2)}, u32[]{:S(2)}) async-start(f32[16,1,72]{2,1,0:T(1,128)} %all_to_all.36), calls=%async_computation.6 | async-start | bytes 16384 | tf_op jit(solution)/shard_map/all_to_all | solution.py:75
  454.2 23.6 %copy-start.1 = (bf16[128,8,768]{2,1,0:T(8,128)(2,1)S(1)}, bf16[128,8,768]{2,1,0:T(8,128)(2,1)}, u32[]{:S(2)}) copy-start(bf16[128,8,768]{2,1,0:T(8,128)(2,1)} %param.5) | copy-start | bytes 4718596
Sparse Core Ops, SparseCore 0:
  300.5 175.2 reduce-scatter.1
